TPU v7x, 256 devices: a whole 4x4x8 slice. The times are simulated.
256 devices in a mesh: head: 8 (over z), vocab: 32 (over y, x, core).
Axes of the slice: x: 4, y: 4, z: 8, core: 2. Of those that a mesh axis runs over, the one named last changes fastest.
Arguments:
- hidden_states: bfloat16 [2048, 8192], P(('head', 'vocab')), may hold values from -6 to 6
- head_weight: bfloat16 [8, 8192, 16384], P('head', None, 'vocab'), may hold values from -1 to 1
- tags: int32 [2048, 1], P(('head', 'vocab')), may hold values from 0 to 7; in each aligned block of 8 rows (0 to 7, 8 to 15, ...) at most 2 rows name the same one
- targets: int32 [2048], P(('head', 'vocab')), may hold values from 0 to 16383
- row_grad: bfloat16 [2048], P(('head', 'vocab')), may hold values from -192 to 192
Outputs:
- row_loss: bfloat16 [2048], P(('head', 'vocab'))
- hidden_grad: bfloat16 [2048, 8192], P(('head', 'vocab'))
Inputs may be any that keep to these rules, and one draw needn't show every extreme that they name: `tags`: in each aligned block of 8 rows (the rows of one device) no head is named by more than 2 rows, and in every draw some block has exactly 2 rows of one head.
All inputs are finite; a program needn't handle non-finite values.
Results may differ from a plain program's by a relative error of at most 0.018.
Values may be sent and summed in bfloat16 or wider, within the bound.
No kernel may reach another device: no remote copies, remote signals or barrier semaphores. Data moves between devices by JAX's collectives and lax.ppermute only.
A program may use at most 64 MiB of HBM per device.

v0:
```python
import jax
import jax.numpy as jnp
from jax import lax
from jax.sharding import PartitionSpec as P

CAP = 2


def project_back(dlog_block, weight):
    return lax.dot_general(
        dlog_block, weight, (((1,), (1,)), ((), ())), preferred_element_type=jnp.float32
    )


def per_device(hidden_states, head_weight, tags, targets, row_grad):
    head_count = lax.axis_size("head")
    own_rows = head_count * CAP
    row_tag = tags[:, 0]
    local_rows = row_tag.shape[0]
    row_iota = lax.broadcasted_iota(jnp.int32, (local_rows, local_rows), 0)
    col_iota = lax.broadcasted_iota(jnp.int32, (local_rows, local_rows), 1)
    earlier = (row_tag[None, :] == row_tag[:, None]) & (col_iota < row_iota)
    slot_rank = jnp.sum(earlier.astype(jnp.int32), axis=1)
    slot_index = row_tag * CAP + slot_rank
    selector = jnp.arange(own_rows, dtype=jnp.int32)[:, None] == slot_index[None, :]
    send_rows = jnp.dot(
        selector.astype(jnp.bfloat16), hidden_states, preferred_element_type=jnp.float32
    ).astype(jnp.bfloat16)
    send_rows = send_rows.reshape(head_count, CAP, hidden_states.shape[1])
    send_targets = jnp.sum(jnp.where(selector, targets[None, :], 0), axis=1).reshape(
        head_count, CAP
    )
    send_scale = (
        jnp.sum(jnp.where(selector, row_grad[None, :].astype(jnp.float32), 0.0), axis=1)
        .astype(jnp.bfloat16)
        .reshape(head_count, CAP)
    )
    arrived = (
        lax.all_to_all(send_rows, "head", split_axis=0, concat_axis=0, tiled=True),
        lax.all_to_all(send_targets, "head", split_axis=0, concat_axis=0, tiled=True),
        lax.all_to_all(send_scale, "head", split_axis=0, concat_axis=0, tiled=True),
    )
    grouped = (
        lax.all_gather(arrived[0], "vocab", axis=0, tiled=True),
        lax.all_gather(arrived[1], "vocab", axis=0, tiled=True),
        lax.all_gather(arrived[2], "vocab", axis=0, tiled=True),
    )
    gathered = grouped[0].reshape(-1, hidden_states.shape[1])
    group_targets = grouped[1].reshape(-1)
    group_scale = grouped[2].reshape(-1).astype(jnp.float32)
    weight = head_weight[0]
    vocab_width = weight.shape[1]
    logits = jnp.dot(gathered, weight, preferred_element_type=jnp.float32)
    offset = lax.axis_index("vocab") * vocab_width
    target_hit = lax.broadcasted_iota(jnp.int32, logits.shape, 1) + offset == group_targets[:, None]
    own_target = jnp.sum(jnp.where(target_hit, logits, 0.0), axis=1)
    row_top = lax.pmax(jnp.max(logits, axis=1), "vocab")
    local_total = jnp.sum(jnp.exp(logits - row_top[:, None]), axis=1)
    row_total, target_logit = lax.psum((local_total, own_target), "vocab")
    group_loss = (jnp.log(row_total) + row_top - target_logit).astype(jnp.bfloat16)
    probabilities = jnp.exp(logits - row_top[:, None]) / row_total[:, None]
    dlogits = (group_scale[:, None] * (probabilities - target_hit.astype(jnp.float32))).astype(
        jnp.bfloat16
    )
    partial_value = project_back(dlogits, weight)
    summed = lax.psum(partial_value.astype(jnp.bfloat16), "vocab").astype(jnp.float32)
    own_grad = lax.dynamic_slice_in_dim(summed, lax.axis_index("vocab") * own_rows, own_rows, 0)
    own_loss = lax.dynamic_slice_in_dim(group_loss, lax.axis_index("vocab") * own_rows, own_rows, 0)
    returned = (
        lax.all_to_all(
            own_grad.astype(jnp.bfloat16).reshape(head_count, CAP, -1),
            "head",
            split_axis=0,
            concat_axis=0,
            tiled=True,
        ),
        lax.all_to_all(
            own_loss.reshape(head_count, CAP), "head", split_axis=0, concat_axis=0, tiled=True
        ),
    )
    back_grad = returned[0].reshape(own_rows, -1)
    back_loss = returned[1].reshape(1, own_rows).astype(jnp.float32)
    hidden_grad = jnp.dot(
        selector.T.astype(jnp.bfloat16), back_grad, preferred_element_type=jnp.float32
    ).astype(jnp.bfloat16)
    row_loss = jnp.sum(jnp.where(selector.T, back_loss, 0.0), axis=1).astype(jnp.bfloat16)
    return (row_loss, hidden_grad)


def solution(mesh):
    placed = (
        P(("head", "vocab"), None),
        P("head", None, "vocab"),
        P(("head", "vocab"), None),
        P(("head", "vocab")),
        P(("head", "vocab")),
    )
    return jax.shard_map(
        per_device,
        mesh=mesh,
        in_specs=placed,
        out_specs=(P(("head", "vocab")), P(("head", "vocab"), None)),
        check_vma=False,
    )
```

profile of v0, /device:TPU:17, one launch (start us, length us, event | category | flops | bytes accessed | tf_op | source)
XLA Modules:
  0.0 415.1 jit_solution(14301299727951055076)
XLA Ops:
  7.2 0.0 copy-start
  7.2 0.0 all-gather.4.cloned.1.call-start
  7.2 0.9 convert_reduce_fusion.2
  8.1 0.7 multiply_add_fusion
  8.8 0.0 copy-done
  8.8 0.3 convolution_convert_fusion.1
  9.1 0.2 reshape.73
  9.3 18.6 %all_to_all.41 = bf16[8,2,8192]{2,1,0:T(2,128)(2,1)} all-to-all(bf16[8,2,8192]{2,1,0:T(2,128)(2,1)S(1)} %reshape.73), channel_id=1, replica_groups=mesh['head'=8,'vocab'=32] {'head'}, dimensions={0} | all-to-all | bytes 524288 | tf_op jit(solution)/shard_map/all_to_all | solution.py:39
  27.9 0.0 all-gather.4.cloned.1.call-update
  28.0 0.7 convert_element_type.77
  28.6 0.1 select_reduce_fusion
  28.7 0.7 convert_element_type.91
  29.4 3.3 all-to-all-start.3
  32.7 0.7 select_reduce_fusion.2
  33.4 0.7 all_to_all.27
  34.1 5.0 %all-to-all-done.3 = bf16[8,1,2]{2,1,0:T(2,128)(2,1)S(1)} async-done(((bf16[8,1,2]{2,1,0:T(2,128)(2,1)}), bf16[8,1,2]{2,1,0:T(2,128)(2,1)S(1)}, u32[]{:S(2)}, u32[]{:S(2)}) %all-to-all-start.3) | async-done | bytes 64 | tf_op jit(solution)/shard_map/all_to_all | solution.py:41
  39.2 3.3 all-to-all-start.1
  42.5 0.0 all-reduce.3.cloned.1.call-start
  42.5 26.8 %all-gather.1 = bf16[256,1,2]{2,1,0:T(2,128)(2,1)S(1)} all-gather(bf16[8,1,2]{2,1,0:T(2,128)(2,1)S(1)} %all-to-all-done.3), channel_id=3, replica_groups=mesh['head'=8,'vocab'=32] {'vocab'}, dimensions={0}, use_global_device_ids=true | all-gather | bytes 1056 | tf_op jit(solution)/shard_map/all_gather | solution.py:46
  69.3 0.4 convert_reduce_fusion
  69.7 0.1 reshape.78
  69.8 0.0 all-to-all-done.1
  69.8 24.3 %all-gather = s32[256,1,2]{2,1,0:T(1,128)S(1)} all-gather(s32[8,1,2]{2,1,0:T(1,128)S(1)} %all-to-all-done.1), channel_id=2, replica_groups=mesh['head'=8,'vocab'=32] {'vocab'}, dimensions={0}, use_global_device_ids=true | all-gather | bytes 2112 | tf_op jit(solution)/shard_map/all_gather | solution.py:45
  94.2 0.5 broadcast.26
  94.7 1.0 reduce.11
  95.6 0.1 eq.52
  95.8 0.0 all-gather.4.cloned.1.call-done
  95.8 13.1 %reshape.74 = bf16[512,8192]{1,0:T(8,128)(2,1)} reshape(bf16[256,2,8192]{2,1,0:T(2,128)(2,1)} %all-gather.4.cloned.1.call-done) | data formatting | bytes 16777216 | tf_op jit(solution)/shard_map/reshape | solution.py:48
  108.9 11.0 %fusion.17 = (f32[512]{0:T(512)S(1)}, f32[512,512]{0,1:T(8,128)S(1)}) fusion(bf16[512,8192]{1,0:T(8,128)(2,1)} %reshape.74, bf16[1,8192,512]{2,1,0:T(8,128)(2,1)} %param.6), kind=kOutput, calls=%fused_computation.35 | convolution fusion | flops 4295228928 | bytes 17827840 | tf_op jit(solution)/shard_map/dot_general | solution.py:53
  119.9 52.5 %pmax.7 = f32[512]{0:T(512)S(1)} all-reduce(f32[512]{0:T(512)S(1)} %get-tuple-element.6), channel_id=1, replica_groups=mesh['head'=8,'vocab'=32] {'vocab'}, use_global_device_ids=true, to_apply=%region_2.3 | all-reduce | flops 512 | bytes 4096 | tf_op jit(solution)/shard_map/pmax | solution.py:57
  172.4 0.3 fusion.7
  172.7 54.8 %all-reduce = (f32[512]{0:T(512)S(1)}, f32[512]{0:T(512)S(1)}) all-reduce(f32[512]{0:T(512)S(1)} %get-tuple-element.3, f32[512]{0:T(512)S(1)} %get-tuple-element.2), channel_id=1, replica_groups=mesh['head'=8,'vocab'=32] {'vocab'}, use_global_device_ids=true, to_apply=%region_7.8 | all-reduce | flops 1024 | bytes 8192 | tf_op jit(solution)/shard_map/psum | solution.py:59
  227.6 10.4 %convolution_convert_fusion = bf16[512,8192]{1,0:T(8,128)(2,1)} fusion(bf16[1,8192,512]{2,1,0:T(8,128)(2,1)} %param.6, f32[512,512]{0,1:T(8,128)S(1)} %get-tuple-element.7, f32[512]{0:T(512)S(1)} %get-tuple-element.5, f32[512]{0:T(512)S(1)} %reshape.78, s32[512]{0:T(512)S(1)} %eq.52, f32[512]{0:T(512)S(1)} %pmax.7, s32[512]{0:T(512)S(1)} %iota_add_fusion), kind=kOutput, calls=%fused_computation | convolution fusion | flops 4300996608 | bytes 17836032 | tf_op jit(solution)/shard_map/dot_general | solution.py:10
  238.0 0.0 all-reduce.3.cloned.1.call-update
  238.0 0.1 dynamic_slice.6
  238.1 0.7 all_to_all.35
  238.8 6.8 %all-to-all-start.2 = ((bf16[8,1,2]{2,1,0:T(2,128)(2,1)}), bf16[8,1,2]{2,1,0:T(2,128)(2,1)S(1)}, u32[]{:S(2)}, u32[]{:S(2)}) async-start(bf16[8,1,2]{2,1,0:T(2,128)(2,1)} %all_to_all.35), calls=%async_computation.2 | async-start | bytes 8192 | tf_op jit(solution)/shard_map/all_to_all | solution.py:77
  245.6 140.7 %all-reduce.3.cloned.1.call-done = bf16[512,8192]{1,0:T(8,128)(2,1)} async-done(((bf16[512,8192]{1,0:T(8,128)(2,1)}), bf16[512,8192]{1,0:T(8,128)(2,1)}) %all-reduce.3.cloned.1.call-update) | async-done | bytes 8388624 | tf_op jit(solution)/shard_map/psum | solution.py:66
  386.3 1.0 convert_convert_fusion
  387.2 0.9 reshape.75
  388.1 0.0 all-to-all-done.2
  388.1 6.7 %all-to-all-start.4 = ((bf16[8,2,8192]{2,1,0:T(2,128)(2,1)}), bf16[8,2,8192]{2,1,0:T(2,128)(2,1)S(1)}, u32[]{:S(2)}, u32[]{:S(2)}) async-start(bf16[8,2,8192]{2,1,0:T(2,128)(2,1)} %reshape.75), calls=%async_computation.4 | async-start | bytes 524288 | tf_op jit(solution)/shard_map/all_to_all | solution.py:70
  394.9 0.1 reshape.77
  395.0 0.7 select_reduce_fusion.1
  395.7 11.6 %all-to-all-done.4 = bf16[8,2,8192]{2,1,0:T(2,128)(2,1)S(1)} async-done(((bf16[8,2,8192]{2,1,0:T(2,128)(2,1)}), bf16[8,2,8192]{2,1,0:T(2,128)(2,1)S(1)}, u32[]{:S(2)}, u32[]{:S(2)}) %all-to-all-start.4) | async-done | bytes 262176 | tf_op jit(solution)/shard_map/all_to_all | solution.py:70
  407.3 0.1 reshape.76
  407.4 0.9 convolution_convert_fusion.2
  (3 shorter events, 0.0 us)
Async XLA Ops:
  7.2 1.6 copy-start
  7.2 88.6 %all-gather.4.cloned.1.call-start = ((), (), s32[]{:S(2)}) async-start(), calls=%async_computation.5 | async-start | bytes 8650752 | tf_op jit(solution)/shard_map/all_gather | solution.py:44
  29.4 9.8 %all-to-all-start.3 = ((bf16[8,1,2]{2,1,0:T(2,128)(2,1)}), bf16[8,1,2]{2,1,0:T(2,128)(2,1)S(1)}, u32[]{:S(2)}, u32[]{:S(2)}) async-start(bf16[8,1,2]{2,1,0:T(2,128)(2,1)} %convert_element_type.91), calls=%async_computation.3 | async-start | bytes 8192 | tf_op jit(solution)/shard_map/all_to_all | solution.py:41
  39.2 30.7 %all-to-all-start.1 = ((s32[8,1,2]{2,1,0:T(1,128)}), s32[8,1,2]{2,1,0:T(1,128)S(1)}, u32[]{:S(2)}, u32[]{:S(2)}) async-start(s32[8,1,2]{2,1,0:T(1,128)} %bitcast.2), calls=%async_computation.1 | async-start | bytes 8192 | tf_op jit(solution)/shard_map/all_to_all | solution.py:40
  42.5 343.8 %all-reduce.3.cloned.1.call-start = ((), (), s32[]{:S(2)}) async-start(), calls=%async_computation.6 | async-start | bytes 16777216 | tf_op jit(solution)/shard_map/psum | solution.py:66
  238.8 149.3 %all-to-all-start.2 = ((bf16[8,1,2]{2,1,0:T(2,128)(2,1)}), bf16[8,1,2]{2,1,0:T(2,128)(2,1)S(1)}, u32[]{:S(2)}, u32[]{:S(2)}) async-start(bf16[8,1,2]{2,1,0:T(2,128)(2,1)} %all_to_all.35), calls=%async_computation.2 | async-start | bytes 8192 | tf_op jit(solution)/shard_map/all_to_all | solution.py:77
  388.1 19.1 %all-to-all-start.4 = ((bf16[8,2,8192]{2,1,0:T(2,128)(2,1)}), bf16[8,2,8192]{2,1,0:T(2,128)(2,1)S(1)}, u32[]{:S(2)}, u32[]{:S(2)}) async-start(bf16[8,2,8192]{2,1,0:T(2,128)(2,1)} %reshape.75), calls=%async_computation.4 | async-start | bytes 524288 | tf_op jit(solution)/shard_map/all_to_all | solution.py:70
Sparse Core Ops, SparseCore 0:
  28.1 56.0 all-gather.3
  238.1 148.1 all-reduce.2
where the time goes:
time: 416 us; the launch traced here: 415 us
  blocking collectives  177 us (43%)
  waiting for transfers between devices  157 us (38%)
  matrix products  22.7 us (5%)
  starting transfers between devices  20.2 us (5%)
  local copies, waits for them, and re-layouts  17.3 us (4%)
  between operations  14.2 us (3%)
  other arithmetic  6.38 us (2%)
    psum x1, waiting for transfers between devices, per_device(): lax.psum(partial_value.astype(jnp.bfloat16), 'vocab').astype(jnp.float32)  141 us
    psum x1, blocking collectives, per_device(): row_total, target_logit = lax.psum((local_total, own_target), 'vocab')  54.8 us
    pmax x1, blocking collectives, per_device(): row_top = lax.pmax(jnp.max(logits, axis=1), 'vocab')  52.5 us
    all_gather x1, blocking collectives, per_device(): lax.all_gather(arrived[2], 'vocab', axis=0, tiled=True)  26.8 us
    all_gather x1, blocking collectives, per_device(): lax.all_gather(arrived[1], 'vocab', axis=0, tiled=True)  24.3 us
    all_to_all x1, blocking collectives, per_device(): lax.all_to_all(send_rows, 'head', split_axis=0, concat_axis=0, tiled=True)  18.6 us
    reshape x1, local copies, waits for them, and re-layouts, per_device(): gathered = grouped[0].reshape(-1, hidden_states.shape[1])  13.1 us
    all_to_all x1, waiting for transfers between devices, per_device(): lax.all_to_all(own_grad.astype(jnp.bfloat16).reshape(head_count, CAP, -1)...  11.6 us
  transfers between devices with their start and end apart: 6, of which 3 were waited for; matrix products, arithmetic and copies ran while one was open for 2% of the time, Pallas kernels for 0%

commit v1 on v0

--- a/solution.py
+++ b/solution.py
@@ -43,7 +43,9 @@
     grouped = (
         lax.all_gather(arrived[0], "vocab", axis=0, tiled=True),
         lax.all_gather(arrived[1], "vocab", axis=0, tiled=True),
-        lax.all_gather(arrived[2], "vocab", axis=0, tiled=True),
+        jnp.concatenate(
+            lax.all_to_all(jnp.stack([arrived[2]] * lax.axis_size("vocab")), "vocab", 0, 0), axis=0
+        ),
     )
     gathered = grouped[0].reshape(-1, hidden_states.shape[1])
     group_targets = grouped[1].reshape(-1)

time: 416 us -> 403 us (0.969)
  blocking collectives: 177 us -> 150 us
  starting transfers between devices: 20.2 us -> 28.3 us
  waiting for transfers between devices: 157 us -> 163 us
    all_gather x1 -> x0, blocking collectives: 26.8 us -> none  [per_device(): lax.all_gather(arrived[2], 'vocab', axis=0, tiled=True)]
    all_to_all x0 -> x1, starting transfers between devices: none -> 11.6 us  [per_device(): lax.all_to_all(jnp.stack([arrived[2]] * lax.axis_size('vocab')), 'vocab',...]
    all_to_all x1, waiting for transfers between devices: 0.01 us -> 6.3 us  [per_device(): lax.all_to_all(send_targets, 'head', split_axis=0, concat_axis=0, tiled=T...]
  transfers between devices with their start and end apart: 6 -> 7, of which waited for: 3 -> 4; matrix products, arithmetic and copies ran while one was open for 2% -> 2% of each run, Pallas kernels for 0% -> 0%
where the time goes in v1:
time: 403 us
  waiting for transfers between devices  163 us (40%)
  blocking collectives  150 us (37%)
  starting transfers between devices  28.3 us (7%)
  matrix products  22.7 us (6%)
  local copies, waits for them, and re-layouts  18.2 us (5%)
  between operations  14.2 us (4%)
  other arithmetic  6 us (1%)
    psum x1, waiting for transfers between devices, per_device(): lax.psum(partial_value.astype(jnp.bfloat16), 'vocab').astype(jnp.float32)  140 us
    psum x1, blocking collectives, per_device(): row_total, target_logit = lax.psum((local_total, own_target), 'vocab')  54.9 us
    pmax x1, blocking collectives, per_device(): row_top = lax.pmax(jnp.max(logits, axis=1), 'vocab')  52.5 us
    all_gather x1, blocking collectives, per_device(): lax.all_gather(arrived[1], 'vocab', axis=0, tiled=True)  24 us
    all_to_all x1, blocking collectives, per_device(): lax.all_to_all(send_rows, 'head', split_axis=0, concat_axis=0, tiled=True)  18.6 us
    reshape x1, local copies, waits for them, and re-layouts, per_device(): gathered = grouped[0].reshape(-1, hidden_states.shape[1])  13.1 us
    all_to_all x1, starting transfers between devices, per_device(): lax.all_to_all(jnp.stack([arrived[2]] * lax.axis_size('vocab')), 'vocab',...  11.6 us
    all_to_all x1, waiting for transfers between devices, per_device(): lax.all_to_all(own_grad.astype(jnp.bfloat16).reshape(head_count, CAP, -1)...  11.6 us
  transfers between devices with their start and end apart: 7, of which 4 were waited for; matrix products, arithmetic and copies ran while one was open for 2% of the time, Pallas kernels for 0%

profile of v1, /device:TPU:17, one launch (start us, length us, event | category | flops | bytes accessed | tf_op | source)
XLA Modules:
  0.0 402.6 jit_solution(208303824269343315)
XLA Ops:
  7.2 0.0 copy-start
  7.2 0.0 all-gather.3.cloned.1.call-start
  7.2 0.9 convert_reduce_fusion.1
  8.1 0.7 multiply_add_fusion
  8.8 0.0 copy-done
  8.8 0.3 convolution_convert_fusion.1
  9.1 0.2 reshape.75
  9.3 18.6 %all_to_all.43 = bf16[8,2,8192]{2,1,0:T(2,128)(2,1)} all-to-all(bf16[8,2,8192]{2,1,0:T(2,128)(2,1)S(1)} %reshape.75), channel_id=1, replica_groups=mesh['head'=8,'vocab'=32] {'head'}, dimensions={0} | all-to-all | bytes 524288 | tf_op jit(solution)/shard_map/all_to_all | solution.py:39
  27.9 0.0 all-gather.3.cloned.1.call-update
  28.0 0.7 convert_element_type.77
  28.6 0.1 select_reduce_fusion
  28.7 0.7 convert_element_type.90
  29.4 3.3 all-to-all-start.3
  32.7 0.7 select_reduce_fusion.2
  33.4 0.7 all_to_all.28
  34.1 5.1 %all-to-all-done.3 = bf16[8,1,2]{2,1,0:T(2,128)(2,1)S(1)} async-done(((bf16[8,1,2]{2,1,0:T(2,128)(2,1)}), bf16[8,1,2]{2,1,0:T(2,128)(2,1)S(1)}, u32[]{:S(2)}, u32[]{:S(2)}) %all-to-all-start.3) | async-done | bytes 64 | tf_op jit(solution)/shard_map/all_to_all | solution.py:41
  39.2 3.3 all-to-all-start.1
  42.5 0.1 copy.29
  42.6 6.3 %all-to-all-done.1 = s32[8,1,2]{2,1,0:T(1,128)S(1)} async-done(((s32[8,1,2]{2,1,0:T(1,128)}), s32[8,1,2]{2,1,0:T(1,128)S(1)}, u32[]{:S(2)}, u32[]{:S(2)}) %all-to-all-start.1) | async-done | bytes 96 | tf_op jit(solution)/shard_map/all_to_all | solution.py:40
  48.9 0.6 stack.5
  49.5 11.6 %all-to-all-start.4 = ((bf16[32,8,2]{1,2,0:T(2,128)(2,1)}), bf16[32,8,2]{1,2,0:T(2,128)(2,1)S(1)}, u32[]{:S(2)}, u32[]{:S(2)}) async-start(bf16[32,8,2]{1,2,0:T(2,128)(2,1)} %stack.5), calls=%async_computation.4 | async-start | bytes 32768 | tf_op jit(solution)/shard_map/all_to_all | solution.py:47
  61.1 0.0 all-reduce.3.cloned.1.call-start
  61.2 24.0 %all-gather = s32[256,1,2]{2,1,0:T(1,128)S(1)} all-gather(s32[8,1,2]{2,1,0:T(1,128)S(1)} %all-to-all-done.1), channel_id=2, replica_groups=mesh['head'=8,'vocab'=32] {'vocab'}, dimensions={0}, use_global_device_ids=true | all-gather | bytes 2112 | tf_op jit(solution)/shard_map/all_gather | solution.py:45
  85.2 0.5 broadcast.24
  85.8 1.0 reduce.7
  86.7 0.1 eq.52
  86.9 0.0 all-to-all-done.4
  86.9 0.1 copy.30
  87.0 0.2 copy.31
  87.1 0.1 reshape.80
  87.3 0.0 all-gather.3.cloned.1.call-done
  87.3 13.1 %reshape.76 = bf16[512,8192]{1,0:T(8,128)(2,1)} reshape(bf16[256,2,8192]{2,1,0:T(2,128)(2,1)} %all-gather.3.cloned.1.call-done) | data formatting | bytes 16777216 | tf_op jit(solution)/shard_map/reshape | solution.py:50
  100.4 11.0 %fusion.17 = (f32[512]{0:T(512)S(1)}, f32[512,512]{0,1:T(8,128)S(1)}) fusion(bf16[512,8192]{1,0:T(8,128)(2,1)} %reshape.76, bf16[1,8192,512]{2,1,0:T(8,128)(2,1)} %param.6), kind=kOutput, calls=%fused_computation.34 | convolution fusion | flops 4295228928 | bytes 17827840 | tf_op jit(solution)/shard_map/dot_general | solution.py:55
  111.4 52.5 %pmax.7 = f32[512]{0:T(512)S(1)} all-reduce(f32[512]{0:T(512)S(1)} %get-tuple-element.6), channel_id=1, replica_groups=mesh['head'=8,'vocab'=32] {'vocab'}, use_global_device_ids=true, to_apply=%region_2.3 | all-reduce | flops 512 | bytes 4096 | tf_op jit(solution)/shard_map/pmax | solution.py:59
  163.9 0.3 fusion.7
  164.2 54.9 %all-reduce = (f32[512]{0:T(512)S(1)}, f32[512]{0:T(512)S(1)}) all-reduce(f32[512]{0:T(512)S(1)} %get-tuple-element.3, f32[512]{0:T(512)S(1)} %get-tuple-element.2), channel_id=1, replica_groups=mesh['head'=8,'vocab'=32] {'vocab'}, use_global_device_ids=true, to_apply=%region_7.8 | all-reduce | flops 1024 | bytes 8192 | tf_op jit(solution)/shard_map/psum | solution.py:61
  219.1 10.4 %convolution_convert_fusion = bf16[512,8192]{1,0:T(8,128)(2,1)} fusion(bf16[1,8192,512]{2,1,0:T(8,128)(2,1)} %param.6, f32[512,512]{0,1:T(8,128)S(1)} %get-tuple-element.7, f32[512]{0:T(512)S(1)} %get-tuple-element.5, f32[512]{0:T(512)S(1)} %reshape.80, s32[512]{0:T(512)S(1)} %eq.52, f32[512]{0:T(512)S(1)} %pmax.7, s32[512]{0:T(512)S(1)} %iota_add_fusion), kind=kOutput, calls=%fused_computation | convolution fusion | flops 4300996608 | bytes 17836032 | tf_op jit(solution)/shard_map/dot_general | solution.py:10
  229.5 0.0 all-reduce.3.cloned.1.call-update
  229.6 0.1 dynamic_slice.6
  229.6 0.7 all_to_all.36
  230.3 3.3 all-to-all-start.2
  233.7 140.1 %all-reduce.3.cloned.1.call-done = bf16[512,8192]{1,0:T(8,128)(2,1)} async-done(((bf16[512,8192]{1,0:T(8,128)(2,1)}), bf16[512,8192]{1,0:T(8,128)(2,1)}) %all-reduce.3.cloned.1.call-update) | async-done | bytes 8388624 | tf_op jit(solution)/shard_map/psum | solution.py:68
  373.8 1.0 convert_convert_fusion
  374.7 0.9 reshape.77
  375.6 0.0 all-to-all-done.2
  375.6 6.7 %all-to-all-start.5 = ((bf16[8,2,8192]{2,1,0:T(2,128)(2,1)}), bf16[8,2,8192]{2,1,0:T(2,128)(2,1)S(1)}, u32[]{:S(2)}, u32[]{:S(2)}) async-start(bf16[8,2,8192]{2,1,0:T(2,128)(2,1)} %reshape.77), calls=%async_computation.5 | async-start | bytes 524288 | tf_op jit(solution)/shard_map/all_to_all | solution.py:72
  382.4 0.1 reshape.79
  382.4 0.7 select_reduce_fusion.1
  383.1 11.6 %all-to-all-done.5 = bf16[8,2,8192]{2,1,0:T(2,128)(2,1)S(1)} async-done(((bf16[8,2,8192]{2,1,0:T(2,128)(2,1)}), bf16[8,2,8192]{2,1,0:T(2,128)(2,1)S(1)}, u32[]{:S(2)}, u32[]{:S(2)}) %all-to-all-start.5) | async-done | bytes 262176 | tf_op jit(solution)/shard_map/all_to_all | solution.py:72
  394.7 0.1 reshape.78
  394.9 0.9 convolution_convert_fusion.2
  (3 shorter events, 0.0 us)
Async XLA Ops:
  7.2 1.6 copy-start
  7.2 80.1 %all-gather.3.cloned.1.call-start = ((), (), s32[]{:S(2)}) async-start(), calls=%async_computation.6 | async-start | bytes 8650752 | tf_op jit(solution)/shard_map/all_gather | solution.py:44
  29.4 9.8 %all-to-all-start.3 = ((bf16[8,1,2]{2,1,0:T(2,128)(2,1)}), bf16[8,1,2]{2,1,0:T(2,128)(2,1)S(1)}, u32[]{:S(2)}, u32[]{:S(2)}) async-start(bf16[8,1,2]{2,1,0:T(2,128)(2,1)} %convert_element_type.90), calls=%async_computation.3 | async-start | bytes 8192 | tf_op jit(solution)/shard_map/all_to_all | solution.py:41
  39.2 9.7 %all-to-all-start.1 = ((s32[8,1,2]{2,1,0:T(1,128)}), s32[8,1,2]{2,1,0:T(1,128)S(1)}, u32[]{:S(2)}, u32[]{:S(2)}) async-start(s32[8,1,2]{2,1,0:T(1,128)} %bitcast.2), calls=%async_computation.1 | async-start | bytes 8192 | tf_op jit(solution)/shard_map/all_to_all | solution.py:40
  49.5 37.4 %all-to-all-start.4 = ((bf16[32,8,2]{1,2,0:T(2,128)(2,1)}), bf16[32,8,2]{1,2,0:T(2,128)(2,1)S(1)}, u32[]{:S(2)}, u32[]{:S(2)}) async-start(bf16[32,8,2]{1,2,0:T(2,128)(2,1)} %stack.5), calls=%async_computation.4 | async-start | bytes 32768 | tf_op jit(solution)/shard_map/all_to_all | solution.py:47
  61.1 312.6 %all-reduce.3.cloned.1.call-start = ((), (), s32[]{:S(2)}) async-start(), calls=%async_computation.7 | async-start | bytes 16777216 | tf_op jit(solution)/shard_map/psum | solution.py:68
  230.3 145.3 %all-to-all-start.2 = ((bf16[8,1,2]{2,1,0:T(2,128)(2,1)}), bf16[8,1,2]{2,1,0:T(2,128)(2,1)S(1)}, u32[]{:S(2)}, u32[]{:S(2)}) async-start(bf16[8,1,2]{2,1,0:T(2,128)(2,1)} %all_to_all.36), calls=%async_computation.2 | async-start | bytes 8192 | tf_op jit(solution)/shard_map/all_to_all | solution.py:79
  375.6 19.1 %all-to-all-start.5 = ((bf16[8,2,8192]{2,1,0:T(2,128)(2,1)}), bf16[8,2,8192]{2,1,0:T(2,128)(2,1)S(1)}, u32[]{:S(2)}, u32[]{:S(2)}) async-start(bf16[8,2,8192]{2,1,0:T(2,128)(2,1)} %reshape.77), calls=%async_computation.5 | async-start | bytes 524288 | tf_op jit(solution)/shard_map/all_to_all | solution.py:72
Sparse Core Ops, SparseCore 0:
  28.1 56.3 all-gather.2
  229.7 144.0 all-reduce.2
